TPU v7x, 128 devices: a whole 4x4x4 slice. The times are simulated.
128 devices in a mesh: mode: 8 (over x, core), member: 16 (over z, y).
Axes of the slice: x: 4, y: 4, z: 4, core: 2. Of those that a mesh axis runs over, the one named last changes fastest.
Arguments:
- ground_accel: bfloat16 [4, 639], replicated, may hold values from -6 to 6
- modal_kernel: bfloat16 [4096, 512], P(('mode', 'member')), may hold values from -0.25 to 0.25
- mode_shapes: bfloat16 [98304, 4096], P('member', 'mode'), may hold values from -0.09375 to 0.09375
- member_owner: int32 [16384, 1], P('member'), may hold values from 0 to 127; in each aligned block of 128 rows (0 to 127, 128 to 255, ...) at most 2 rows name the same one
- member_group: int32 [16384, 1], P('member'), may hold values from 0 to 3
- record_table: int32 [512, 8], P(('mode', 'member')), may hold values from 0 to 3
- case_coef: float32 [8, 6], replicated, may hold values from -1.5 to 1.5
- gravity: float32 [512, 8], P(('mode', 'member')), may hold values from -10 to 10
Outputs:
- demand: float32 [512, 8], P(('mode', 'member'))
Inputs may be any that keep to these rules, and one draw needn't show every extreme that they name: `member_owner`: in each aligned block of 1024 / 8 members no owner is named more than 2 times, a bound that some block reaches.
All inputs are finite; a program needn't handle non-finite values.
Results may differ from a plain program's by a relative error of at most 0.0065.
Values may be sent and summed in bfloat16 or wider, within the bound.
No kernel may reach another device: no remote copies, remote signals or barrier semaphores. Data moves between devices by JAX's collectives and lax.ppermute only.
A program may use at most 64 MiB of HBM per device.

v0:
```python
import jax
import jax.numpy as jnp
from jax import lax
from jax.sharding import PartitionSpec as P


def lagged_table(ground_accel, tap_count):
    record_count, span_len = ground_accel.shape
    step_count = span_len - tap_count + 1
    tiled = jnp.tile(ground_accel, (1, step_count + 1))[:, : step_count * (span_len + 1)]
    windows = tiled.reshape(record_count, step_count, span_len + 1)[:, :, :tap_count]
    return windows.reshape(record_count * step_count, tap_count)


def local(
    ground_accel,
    modal_kernel,
    mode_shapes,
    member_owner,
    member_group,
    record_table,
    case_coef,
    gravity,
):
    tap_count = modal_kernel.shape[1]
    record_count = ground_accel.shape[0]
    comp_count = case_coef.shape[1]
    group_count = gravity.shape[0]
    n_mode = lax.axis_size("mode")
    n_member = lax.axis_size("member")
    lagged = lagged_table(ground_accel, tap_count)
    local_resp = lax.dot_general(
        modal_kernel[:, ::-1], lagged, (((1,), (1,)), ((), ())), preferred_element_type=jnp.float32
    ).astype(jnp.bfloat16)
    modal_resp = lax.all_gather(local_resp, "member", axis=0, tiled=True)
    own_rows = mode_shapes.shape[0] // n_mode
    forces = lax.psum_scatter(
        jnp.dot(mode_shapes, modal_resp, preferred_element_type=jnp.float32).astype(jnp.bfloat16),
        "mode",
        scatter_dimension=0,
        tiled=True,
    ).astype(jnp.float32)
    members_here = own_rows // comp_count
    owner_total = n_mode * n_member
    slot_depth = max(2, 2 * members_here // owner_total)
    packed = forces.reshape(members_here, comp_count * forces.shape[1])
    first_row = lax.axis_index("mode") * members_here
    owner_ids = lax.dynamic_slice_in_dim(member_owner[:, 0], first_row, members_here)
    group_ids = lax.dynamic_slice_in_dim(member_group[:, 0], first_row, members_here)
    position = jnp.arange(members_here)
    earlier = (owner_ids[:, None] == owner_ids[None, :]) & (position[None, :] < position[:, None])
    member_rank = jnp.sum(earlier.astype(jnp.int32), axis=1)
    slot_index = owner_ids * slot_depth + member_rank
    slot_total = owner_total * slot_depth
    placement = jnp.arange(slot_total)[:, None] == slot_index[None, :]
    outgoing = jnp.dot(placement.astype(jnp.float32), packed, precision=lax.Precision.HIGHEST)
    slot_labels = jnp.max(jnp.where(placement, group_ids[None, :], -1), axis=1)
    incoming, slot_tags = (
        lax.all_to_all(
            outgoing.reshape(owner_total, slot_depth, -1).astype(jnp.bfloat16),
            ("mode", "member"),
            split_axis=0,
            concat_axis=0,
            tiled=True,
        ).astype(jnp.float32),
        lax.all_to_all(
            slot_labels.reshape(owner_total, slot_depth),
            ("mode", "member"),
            split_axis=0,
            concat_axis=0,
            tiled=True,
        ),
    )
    selector = (jnp.arange(group_count)[:, None] == slot_tags.reshape(-1)[None, :]).astype(
        jnp.float32
    )
    group_sums = jnp.dot(
        selector, incoming.reshape(selector.shape[1], -1), precision=lax.Precision.HIGHEST
    )
    group_sums = group_sums.reshape(group_count, comp_count, record_count, -1)
    case_mix = jnp.einsum("sc,gcrt->gsrt", case_coef, group_sums, precision=lax.Precision.HIGHEST)
    record_pick = (record_table[:, :, None] == jnp.arange(record_count)[None, None, :]).astype(
        jnp.float32
    )
    selected = jnp.sum(record_pick[:, :, :, None] * case_mix, axis=2)
    combined = gravity[:, :, None] + selected
    return jnp.max(jnp.abs(combined), axis=2)


def solution(mesh):
    placed = (
        P(),
        P(("mode", "member"), None),
        P("member", "mode"),
        P("member", None),
        P("member", None),
        P(("mode", "member"), None),
        P(),
        P(("mode", "member"), None),
    )
    return jax.shard_map(
        local, mesh=mesh, in_specs=placed, out_specs=P(("mode", "member"), None), check_vma=False
    )
```

profile of v0, /device:TPU:1, one launch (start us, length us, event | category | flops | bytes accessed | tf_op | source)
XLA Modules:
  0.0 134.6 jit_solution(4952856009396040289)
XLA Ops:
  6.5 0.0 copy-start
  6.5 0.0 reduce-scatter.2.cloned.1.call-start
  6.5 1.6 %rev.3 = bf16[32,512]{1,0:T(8,128)(2,1)S(1)} reverse(bf16[32,512]{1,0:T(8,128)(2,1)} %param.9), dimensions={1} | reverse | bytes 65536 | tf_op jit(solution)/shard_map/rev | solution.py:33
  8.2 0.7 tile.4
  8.9 0.6 tile.10
  9.6 0.2 slice.8
  9.8 0.1 copy.27
  9.9 0.2 convolution_convert_fusion.2
  10.2 21.2 %all_gather.3 = bf16[512,512]{1,0:T(8,128)(2,1)S(1)} all-gather(bf16[32,512]{1,0:T(8,128)(2,1)S(1)} %convolution_convert_fusion.2), channel_id=1, replica_groups=mesh['mode'=8,'member'=16] {'member'}, dimensions={0}, use_global_device_ids=true | all-gather | bytes 557056 | tf_op jit(solution)/shard_map/all_gather | solution.py:35
  31.4 8.3 %fusion = bf16[6144,512]{0,1:T(8,128)(2,1)} fusion(bf16[512,512]{1,0:T(8,128)(2,1)S(1)} %all_gather.3, bf16[6144,512]{1,0:T(8,128)(2,1)} %param.10), kind=kOutput, calls=%fused_computation.1 | convolution fusion | flops 3224371200 | bytes 13107200 | tf_op jit(solution)/shard_map/dot_general | solution.py:38
  39.6 0.0 reduce-scatter.2.cloned.1.call-update
  39.7 0.7 dynamic-slice_bitcast_fusion.1
  40.3 0.7 dynamic-slice_bitcast_fusion
  41.0 0.2 convert_reduce_fusion
  41.2 0.7 multiply_add_fusion.1
  41.8 0.1 select_reduce_fusion
  41.9 0.8 all_to_all.9
  42.7 12.8 %all-to-all-start = ((s32[128,1,2]{2,1,0:T(1,128)}), s32[128,1,2]{2,1,0:T(1,128)S(1)}, u32[]{:S(2)}, u32[]{:S(2)}) async-start(s32[128,1,2]{2,1,0:T(1,128)} %bitcast.2), calls=%async_computation | async-start | bytes 131072 | tf_op jit(solution)/shard_map/all_to_all | solution.py:66
  55.5 31.4 %reduce-scatter.2.cloned.1.call-done = bf16[768,512]{0,1:T(8,128)(2,1)} async-done(((bf16[6144,512]{0,1:T(8,128)(2,1)}), bf16[768,512]{0,1:T(8,128)(2,1)}) %reduce-scatter.2.cloned.1.call-update) | async-done | bytes 786448 | tf_op jit(solution)/shard_map/reduce_scatter | solution.py:37
  86.9 1.4 %copy.17 = bf16[768,512]{1,0:T(8,128)(2,1)S(1)} copy(bf16[768,512]{0,1:T(8,128)(2,1)} %reduce-scatter.2.cloned.1.call-done) | data formatting | bytes 1572864 | tf_op jit(solution)/shard_map/reduce_scatter | solution.py:37
  88.3 0.7 reshape.68
  89.0 0.6 convolution_convert_fusion.1
  89.6 2.8 %copy.18 = bf16[128,2,3072]{2,1,0:T(2,128)(2,1)} copy(bf16[128,2,3072]{2,0,1:T(8,128)(2,1)S(1)} %convolution_convert_fusion.1) | data formatting | bytes 3145728 | tf_op jit(solution)/shard_map/convert_element_type | solution.py:60
  92.4 0.0 copy-start.1
  92.4 0.0 all-to-all-done
  92.4 8.5 %all-to-all-start.1 = ((bf16[128,2,3072]{2,1,0:T(2,128)(2,1)}), bf16[128,2,3072]{2,1,0:T(2,128)(2,1)S(1)}, u32[]{:S(2)}, u32[]{:S(2)}) async-start(bf16[128,2,3072]{2,1,0:T(2,128)(2,1)} %copy.18), calls=%async_computation.2 | async-start | bytes 3145728 | tf_op jit(solution)/shard_map/all_to_all | solution.py:59
  100.9 0.0 copy-done.1
  100.9 0.5 broadcast.35
  101.4 0.8 reduce.3
  102.2 0.1 eq.85
  102.4 22.6 %all-to-all-done.1 = bf16[128,2,3072]{2,1,0:T(2,128)(2,1)S(1)} async-done(((bf16[128,2,3072]{2,1,0:T(2,128)(2,1)}), bf16[128,2,3072]{2,1,0:T(2,128)(2,1)S(1)}, u32[]{:S(2)}, u32[]{:S(2)}) %all-to-all-start.1) | async-done | bytes 1572896 | tf_op jit(solution)/shard_map/all_to_all | solution.py:59
  125.0 0.6 reshape.67
  125.6 0.7 copy.19
  126.3 0.0 copy-start.2
  126.3 0.5 fusion.11
  126.8 0.0 copy-done
  126.8 0.2 fusion.2
  127.0 0.0 copy-done.2
  127.0 0.7 abs_reduce_fusion
  (3 shorter events, 0.0 us)
Async XLA Ops:
  6.5 120.3 %copy-start = (f32[8,6]{1,0:T(8,128)S(1)}, f32[8,6]{1,0:T(8,128)}, u32[]{:S(2)}) copy-start(f32[8,6]{1,0:T(8,128)} %param.14) | copy-start | bytes 580
  6.5 80.3 %reduce-scatter.2.cloned.1.call-start = ((), (), s32[]{:S(2)}) async-start(), calls=%async_computation.3 | async-start | bytes 7077888 | tf_op jit(solution)/shard_map/reduce_scatter | solution.py:37
  42.7 49.7 %all-to-all-start = ((s32[128,1,2]{2,1,0:T(1,128)}), s32[128,1,2]{2,1,0:T(1,128)S(1)}, u32[]{:S(2)}, u32[]{:S(2)}) async-start(s32[128,1,2]{2,1,0:T(1,128)} %bitcast.2), calls=%async_computation | async-start | bytes 131072 | tf_op jit(solution)/shard_map/all_to_all | solution.py:66
  92.4 8.5 %copy-start.1 = (s32[4,8]{1,0:T(4,128)S(1)}, s32[4,8]{1,0:T(4,128)}, u32[]{:S(2)}) copy-start(s32[4,8]{1,0:T(4,128)} %param.13) | copy-start | bytes 388
  92.4 32.6 %all-to-all-start.1 = ((bf16[128,2,3072]{2,1,0:T(2,128)(2,1)}), bf16[128,2,3072]{2,1,0:T(2,128)(2,1)S(1)}, u32[]{:S(2)}, u32[]{:S(2)}) async-start(bf16[128,2,3072]{2,1,0:T(2,128)(2,1)} %copy.18), calls=%async_computation.2 | async-start | bytes 3145728 | tf_op jit(solution)/shard_map/all_to_all | solution.py:59
  126.3 0.7 copy-start.2
Sparse Core Ops, SparseCore 0:
  39.8 47.0 reduce-scatter.1
where the time goes:
time: 135 us
  waiting for transfers between devices  54 us (40%)
  starting transfers between devices  21.3 us (16%)
  blocking collectives  21.2 us (16%)
  between operations  13.5 us (10%)
  local copies, waits for them, and re-layouts  12.3 us (9%)
  matrix products  9.84 us (7%)
  other arithmetic  2.5 us (2%)
    reduce_scatter x1, waiting for transfers between devices, local(): lax.psum_scatter(jnp.dot(mode_shapes, modal_resp, preferred_element_type=...  31.4 us
    all_to_all x1, waiting for transfers between devices, local(): lax.all_to_all(outgoing.reshape(owner_total, slot_depth, -1).astype(jnp.b...  22.6 us
    all_gather x1, blocking collectives, local(): modal_resp = lax.all_gather(local_resp, 'member', axis=0, tiled=True)  21.2 us
    all_to_all x1, starting transfers between devices, local(): lax.all_to_all(slot_labels.reshape(owner_total, slot_depth), ('mode', 'me...  12.8 us
    all_to_all x1, starting transfers between devices, local(): lax.all_to_all(outgoing.reshape(owner_total, slot_depth, -1).astype(jnp.b...  8.52 us
    dot_general x1, matrix products, local(): jnp.dot(mode_shapes, modal_resp, preferred_element_type=jnp.float32)  8.28 us
    convert_element_type x1, local copies, waits for them, and re-layouts, local(): outgoing.reshape(owner_total, slot_depth, -1).astype(jnp.bfloat16)  2.77 us
  transfers between devices with their start and end apart: 3, of which 2 were waited for; matrix products, arithmetic and copies ran while one was open for 7% of the time, Pallas kernels for 0%

commit v1 on v0

--- a/solution.py
+++ b/solution.py
@@ -32,7 +32,9 @@
     local_resp = lax.dot_general(
         modal_kernel[:, ::-1], lagged, (((1,), (1,)), ((), ())), preferred_element_type=jnp.float32
     ).astype(jnp.bfloat16)
-    modal_resp = lax.all_gather(local_resp, "member", axis=0, tiled=True)
+    modal_resp = jnp.concatenate(
+        lax.all_to_all(jnp.stack([local_resp] * lax.axis_size("member")), "member", 0, 0), axis=0
+    )
     own_rows = mode_shapes.shape[0] // n_mode
     forces = lax.psum_scatter(
         jnp.dot(mode_shapes, modal_resp, preferred_element_type=jnp.float32).astype(jnp.bfloat16),

time: 135 us -> 127 us (0.941)
  starting transfers between devices: 21.3 us -> 15.6 us
  blocking collectives: 21.2 us -> 18.9 us
    all_gather x1 -> x0, blocking collectives: 21.2 us -> none  [local(): modal_resp = lax.all_gather(local_resp, 'member', axis=0, tiled=True)]
    all_to_all x0 -> x1, blocking collectives: none -> 18.9 us  [local(): lax.all_to_all(jnp.stack([local_resp] * lax.axis_size('member')), 'member...]
    all_to_all x1, starting transfers between devices: 12.8 us -> 7.07 us  [local(): lax.all_to_all(slot_labels.reshape(owner_total, slot_depth), ('mode', 'me...]
where the time goes in v1:
time: 127 us
  waiting for transfers between devices  54 us (43%)
  blocking collectives  18.9 us (15%)
  starting transfers between devices  15.6 us (12%)
  between operations  13.6 us (11%)
  local copies, waits for them, and re-layouts  12.3 us (10%)
  matrix products  9.83 us (8%)
  other arithmetic  2.5 us (2%)
    reduce_scatter x1, waiting for transfers between devices, local(): lax.psum_scatter(jnp.dot(mode_shapes, modal_resp, preferred_element_type=...  31.4 us
    all_to_all x1, waiting for transfers between devices, local(): lax.all_to_all(outgoing.reshape(owner_total, slot_depth, -1).astype(jnp.b...  22.6 us
    all_to_all x1, blocking collectives, local(): lax.all_to_all(jnp.stack([local_resp] * lax.axis_size('member')), 'member...  18.9 us
    all_to_all x1, starting transfers between devices, local(): lax.all_to_all(outgoing.reshape(owner_total, slot_depth, -1).astype(jnp.b...  8.51 us
    dot_general x1, matrix products, local(): jnp.dot(mode_shapes, modal_resp, preferred_element_type=jnp.float32)  8.27 us
    all_to_all x1, starting transfers between devices, local(): lax.all_to_all(slot_labels.reshape(owner_total, slot_depth), ('mode', 'me...  7.07 us
    convert_element_type x1, local copies, waits for them, and re-layouts, local(): outgoing.reshape(owner_total, slot_depth, -1).astype(jnp.bfloat16)  2.77 us
  transfers between devices with their start and end apart: 3, of which 2 were waited for; matrix products, arithmetic and copies ran while one was open for 7% of the time, Pallas kernels for 0%

profile of v1, /device:TPU:1, one launch (start us, length us, event | category | flops | bytes accessed | tf_op | source)
XLA Modules:
  0.0 126.7 jit_solution(8161426989656635601)
XLA Ops:
  6.5 0.0 copy-start
  6.5 0.0 reduce-scatter.2.cloned.1.call-start
  6.5 1.6 %rev.3 = bf16[32,512]{1,0:T(8,128)(2,1)S(1)} reverse(bf16[32,512]{1,0:T(8,128)(2,1)} %param.9), dimensions={1} | reverse | bytes 65536 | tf_op jit(solution)/shard_map/rev | solution.py:33
  8.2 0.7 tile.4
  8.9 0.6 tile.10
  9.6 0.2 slice.8
  9.8 0.1 copy.27
  9.9 0.2 convolution_convert_fusion.2
  10.2 0.1 stack.2
  10.3 18.9 %all_to_all.19 = bf16[16,32,512]{2,1,0:T(8,128)(2,1)S(1)} all-to-all(bf16[16,32,512]{2,1,0:T(8,128)(2,1)S(1)} %stack.2), channel_id=1, replica_groups=mesh['mode'=8,'member'=16] {'member'}, dimensions={0} | all-to-all | bytes 1048576 | tf_op jit(solution)/shard_map/all_to_all | solution.py:36
  29.2 8.3 %fusion = bf16[6144,512]{0,1:T(8,128)(2,1)} fusion(bf16[512,512]{1,0:T(8,128)(2,1)S(1)} %bitcast.44, bf16[6144,512]{1,0:T(8,128)(2,1)} %param.10), kind=kOutput, calls=%fused_computation.1 | convolution fusion | flops 3224371200 | bytes 13107200 | tf_op jit(solution)/shard_map/dot_general | solution.py:40
  37.4 0.0 reduce-scatter.2.cloned.1.call-update
  37.5 0.7 dynamic-slice_bitcast_fusion.1
  38.1 0.7 dynamic-slice_bitcast_fusion
  38.8 0.2 convert_reduce_fusion
  39.0 0.7 multiply_add_fusion.1
  39.6 0.1 select_reduce_fusion
  39.7 0.8 all_to_all.12
  40.5 7.1 %all-to-all-start = ((s32[128,1,2]{2,1,0:T(1,128)}), s32[128,1,2]{2,1,0:T(1,128)S(1)}, u32[]{:S(2)}, u32[]{:S(2)}) async-start(s32[128,1,2]{2,1,0:T(1,128)} %bitcast.2), calls=%async_computation | async-start | bytes 131072 | tf_op jit(solution)/shard_map/all_to_all | solution.py:68
  47.6 31.4 %reduce-scatter.2.cloned.1.call-done = bf16[768,512]{0,1:T(8,128)(2,1)} async-done(((bf16[6144,512]{0,1:T(8,128)(2,1)}), bf16[768,512]{0,1:T(8,128)(2,1)}) %reduce-scatter.2.cloned.1.call-update) | async-done | bytes 786448 | tf_op jit(solution)/shard_map/reduce_scatter | solution.py:39
  79.0 1.4 %copy.17 = bf16[768,512]{1,0:T(8,128)(2,1)S(1)} copy(bf16[768,512]{0,1:T(8,128)(2,1)} %reduce-scatter.2.cloned.1.call-done) | data formatting | bytes 1572864 | tf_op jit(solution)/shard_map/reduce_scatter | solution.py:39
  80.4 0.7 reshape.74
  81.1 0.6 convolution_convert_fusion.1
  81.7 2.8 %copy.18 = bf16[128,2,3072]{2,1,0:T(2,128)(2,1)} copy(bf16[128,2,3072]{2,0,1:T(8,128)(2,1)S(1)} %convolution_convert_fusion.1) | data formatting | bytes 3145728 | tf_op jit(solution)/shard_map/convert_element_type | solution.py:62
  84.5 0.0 copy-start.1
  84.5 0.0 all-to-all-done
  84.5 8.5 %all-to-all-start.2 = ((bf16[128,2,3072]{2,1,0:T(2,128)(2,1)}), bf16[128,2,3072]{2,1,0:T(2,128)(2,1)S(1)}, u32[]{:S(2)}, u32[]{:S(2)}) async-start(bf16[128,2,3072]{2,1,0:T(2,128)(2,1)} %copy.18), calls=%async_computation.3 | async-start | bytes 3145728 | tf_op jit(solution)/shard_map/all_to_all | solution.py:61
  93.0 0.0 copy-done.1
  93.0 0.5 broadcast.37
  93.5 0.8 reduce.3
  94.3 0.1 eq.85
  94.5 22.6 %all-to-all-done.2 = bf16[128,2,3072]{2,1,0:T(2,128)(2,1)S(1)} async-done(((bf16[128,2,3072]{2,1,0:T(2,128)(2,1)}), bf16[128,2,3072]{2,1,0:T(2,128)(2,1)S(1)}, u32[]{:S(2)}, u32[]{:S(2)}) %all-to-all-start.2) | async-done | bytes 1572896 | tf_op jit(solution)/shard_map/all_to_all | solution.py:61
  117.1 0.6 reshape.73
  117.7 0.7 copy.19
  118.4 0.0 copy-start.2
  118.4 0.5 fusion.11
  118.9 0.0 copy-done
  118.9 0.2 fusion.2
  119.1 0.0 copy-done.2
  119.2 0.7 abs_reduce_fusion
  (3 shorter events, 0.0 us)
Async XLA Ops:
  6.5 112.4 %copy-start = (f32[8,6]{1,0:T(8,128)S(1)}, f32[8,6]{1,0:T(8,128)}, u32[]{:S(2)}) copy-start(f32[8,6]{1,0:T(8,128)} %param.14) | copy-start | bytes 580
  6.5 72.5 %reduce-scatter.2.cloned.1.call-start = ((), (), s32[]{:S(2)}) async-start(), calls=%async_computation.4 | async-start | bytes 7077888 | tf_op jit(solution)/shard_map/reduce_scatter | solution.py:39
  40.5 44.0 %all-to-all-start = ((s32[128,1,2]{2,1,0:T(1,128)}), s32[128,1,2]{2,1,0:T(1,128)S(1)}, u32[]{:S(2)}, u32[]{:S(2)}) async-start(s32[128,1,2]{2,1,0:T(1,128)} %bitcast.2), calls=%async_computation | async-start | bytes 131072 | tf_op jit(solution)/shard_map/all_to_all | solution.py:68
  84.5 8.5 %copy-start.1 = (s32[4,8]{1,0:T(4,128)S(1)}, s32[4,8]{1,0:T(4,128)}, u32[]{:S(2)}) copy-start(s32[4,8]{1,0:T(4,128)} %param.13) | copy-start | bytes 388
  84.5 32.6 %all-to-all-start.2 = ((bf16[128,2,3072]{2,1,0:T(2,128)(2,1)}), bf16[128,2,3072]{2,1,0:T(2,128)(2,1)S(1)}, u32[]{:S(2)}, u32[]{:S(2)}) async-start(bf16[128,2,3072]{2,1,0:T(2,128)(2,1)} %copy.18), calls=%async_computation.3 | async-start | bytes 3145728 | tf_op jit(solution)/shard_map/all_to_all | solution.py:61
  118.4 0.7 copy-start.2
Sparse Core Ops, SparseCore 0:
  37.6 41.3 reduce-scatter.1
